TPU v7x, 512 devices: a whole 4x4x16 slice. The times are simulated.
512 devices in a mesh: src: 16 (over z_hi, x), dst: 32 (over z_lo, y, core).
Axes of the slice: x: 4, y: 4, z: 16 (z_hi: 4, z_lo: 4; z = z_hi * 4 + z_lo), core: 2. Of those that a mesh axis runs over, the one named last changes fastest.
Arguments:
- rel_ops: bfloat16 [2048, 400, 400], P(('src', 'dst')), may hold values from -0.3125 to 0.3125
- src_emb: bfloat16 [4096, 400], P('src'), may hold values from -1.796875 to 1.796875
- dst_emb: bfloat16 [8192, 400], P('dst'), may hold values from -6 to 6
- edge_src: int32 [16, 32, 1024], P('src', 'dst'), may hold values from 0 to 255
- edge_dst: int32 [16, 32, 1024], P('src', 'dst'), may hold values from 0 to 255
- slot_count: int32 [16, 32, 64], P('src', 'dst'), may hold values from 0 to 16
- neg_span: int32 [16, 2], P('src'), may hold values from 0 to 31
Outputs:
- grad_rel: bfloat16 [2048, 400, 400], P(('src', 'dst'))
- grad_src: bfloat16 [4096, 400], P('src')
- grad_dst: bfloat16 [8192, 400], P('dst')
All inputs are finite; a program needn't handle non-finite values.
Results may differ from a plain program's by a relative error of at most 0.015.
Values may be sent and summed in bfloat16 or wider, within the bound.
No kernel may reach another device: no remote copies, remote signals or barrier semaphores. Data moves between devices by JAX's collectives and lax.ppermute only.
A program may use at most 64 MiB of HBM per device.

v0:
```python
import jax
import jax.numpy as jnp
from jax import lax
from jax.sharding import PartitionSpec as P


def from_root(block, axis, holder):
    block = jnp.where(lax.axis_index(axis) == holder, block, jnp.zeros_like(block))
    return lax.psum(block, axis)


def send_back(rows_out):
    return lax.all_to_all(rows_out, "src", split_axis=0, concat_axis=0, tiled=True)


def body(rel_ops, src_emb, dst_emb, edge_src, edge_dst, slot_count, neg_span):
    n_src = lax.axis_size("src")
    rel_count = rel_ops.shape[0]
    model_width = rel_ops.shape[1]
    part_rows = src_emb.shape[0]
    slot_total = edge_src.shape[2]
    slot_cap = slot_total // (n_src * rel_count)
    ids_src = edge_src.reshape(slot_total)
    ids_dst = edge_dst.reshape(slot_total)
    counts = slot_count.reshape(n_src * rel_count)
    slot_lane = jnp.arange(slot_total, dtype=jnp.int32) % slot_cap
    live_mask = (slot_lane < jnp.repeat(counts, slot_cap, total_repeat_length=slot_total)).astype(
        jnp.float32
    )
    inputs = src_emb[ids_src].reshape(n_src, rel_count, slot_cap, model_width)
    received = lax.all_to_all(inputs, "src", split_axis=0, concat_axis=0, tiled=True)
    applied = jnp.einsum(
        "skcd,kde->skce", received, rel_ops, preferred_element_type=jnp.float32
    ).astype(jnp.bfloat16)
    mapped = lax.all_to_all(applied, "src", split_axis=0, concat_axis=0, tiled=True)
    mapped_rows = mapped.reshape(slot_total, model_width)
    targets = dst_emb[ids_dst]
    span_ids = neg_span.reshape(-1)
    span_total = span_ids.shape[0]
    pieces = [from_root(dst_emb, "dst", span_ids[index]) for index in range(span_total)]
    negatives = jnp.concatenate(pieces, 0)
    block_rows = min(512, slot_total)
    block_count = slot_total // block_rows

    def block_step(span_acc, block_in):
        rows_z, rows_y, rows_live = block_in
        neg_score = jnp.einsum("bd,nd->bn", rows_z, negatives, preferred_element_type=jnp.float32)
        pos_score = jnp.sum(rows_z.astype(jnp.float32) * rows_y.astype(jnp.float32), -1)
        row_max = jnp.maximum(jnp.max(neg_score, -1), pos_score)
        exp_neg = jnp.exp(neg_score - row_max[:, None])
        exp_pos = jnp.exp(pos_score - row_max)
        denom = jnp.sum(exp_neg, -1) + exp_pos
        grad_neg = (exp_neg * (rows_live / denom)[:, None]).astype(jnp.bfloat16)
        grad_pos = (exp_pos / denom - 1.0) * rows_live
        upstream = grad_pos[:, None] * rows_y.astype(jnp.float32) + jnp.dot(
            grad_neg, negatives, preferred_element_type=jnp.float32
        )
        dst_term = grad_pos[:, None] * rows_z.astype(jnp.float32)
        span_acc = span_acc + jnp.einsum(
            "bn,bd->nd", grad_neg, rows_z, preferred_element_type=jnp.float32
        )
        return (span_acc, (upstream.astype(jnp.bfloat16), dst_term))

    span_start = jnp.zeros((span_total * part_rows, model_width), jnp.float32)
    scanned = (
        mapped_rows.reshape(block_count, block_rows, model_width),
        targets.reshape(block_count, block_rows, model_width),
        live_mask.reshape(block_count, block_rows),
    )
    span_grad, (up_blocks, dst_blocks) = lax.scan(block_step, span_start, scanned)
    grads_out = up_blocks.reshape(n_src, rel_count, slot_cap, model_width)
    received = (
        lax.all_to_all(grads_out, "src", split_axis=0, concat_axis=0, tiled=True),
        lax.all_to_all(inputs, "src", split_axis=0, concat_axis=0, tiled=True),
    )
    grads_in = send_back(
        jnp.einsum(
            "skce,kde->skcd", received[0], rel_ops, preferred_element_type=jnp.float32
        ).astype(jnp.bfloat16)
    )
    grads_recv = received[0]
    inputs_recv = received[1]
    grad_rel = jnp.einsum(
        "skcd,skce->kde", inputs_recv, grads_recv, preferred_element_type=jnp.float32
    ).astype(jnp.bfloat16)
    src_local = jax.ops.segment_sum(
        grads_in.reshape(slot_total, model_width).astype(jnp.float32),
        ids_src,
        num_segments=part_rows,
    )
    grad_src = lax.psum(src_local, "dst").astype(jnp.bfloat16)
    span_sums = (
        lax.psum(span_grad.astype(jnp.bfloat16), "dst")
        .astype(jnp.float32)
        .reshape(span_total, part_rows, model_width)
    )
    own_index = lax.axis_index("dst")
    dst_local = jax.ops.segment_sum(
        dst_blocks.reshape(slot_total, model_width), ids_dst, num_segments=part_rows
    )
    for index in range(span_total):
        dst_local = dst_local + jnp.where(span_ids[index] == own_index, span_sums[index], 0.0)
    grad_dst = lax.psum(dst_local, "src").astype(jnp.bfloat16)
    return (grad_rel, grad_src, grad_dst)


def solution(mesh):
    placed = (
        P(("src", "dst"), None, None),
        P("src", None),
        P("dst", None),
        P("src", "dst", None),
        P("src", "dst", None),
        P("src", "dst", None),
        P("src", None),
    )
    return jax.shard_map(
        body,
        mesh=mesh,
        in_specs=placed,
        out_specs=(P(("src", "dst"), None, None), P("src", None), P("dst", None)),
        check_vma=False,
    )
```

profile of v0, /device:TPU:384, one launch (start us, length us, event | category | flops | bytes accessed | tf_op | source)
XLA Modules:
  0.0 1055.3 jit_solution(10922361248387512830)
XLA Ops:
  7.2 0.8 compare_select_fusion.2
  8.0 1.1 copy.68
  9.1 5.1 gather_fusion
  14.2 64.1 %all_to_all.21 = bf16[16,4,16,400]{3,2,1,0:T(8,128)(2,1)S(1)} all-to-all(bf16[16,4,16,400]{3,2,1,0:T(8,128)(2,1)} %bitcast.146), channel_id=1, replica_groups=mesh['src'=16,'dst'=32] {'src'}, dimensions={0} | all-to-all | bytes 1638400 | tf_op jit(solution)/shard_map/all_to_all | solution.py:74
  78.3 0.7 fusion.27
  79.0 0.3 copy-done.6
  79.3 1.1 copy.70
  80.4 9.5 all-to-all-start.1
  90.0 0.6 fusion.40
  91.8 0.1 copy.71
  92.0 0.8 broadcast_select_fusion.1
  92.9 0.7 fusion.39
  93.6 0.7 fusion.37
  94.3 0.7 fusion.38
  95.0 0.7 fusion.36
  95.8 4.3 compare_select_fusion.3
  100.2 0.7 compare_reduce_fusion.56
  100.9 35.6 %select_select_fusion = s32[1024]{0:T(1024)S(1)} fusion(pred[1024]{0:T(1024)(128)(4,1)S(1)} %get-tuple-element.256, pred[1024]{0:T(1024)(128)(4,1)S(1)} %get-tuple-element.255, pred[1024]{0:T(1024)(128)(4,1)S(1)} %get-tuple-element.254, pred[1024]{0:T(1024)(128)(4,1)S(1)} %get-tuple-element.253, pred[1024]{0:T(1024)(128)(4,1)S(1)} %get-tuple-element.252, ...), kind=kLoop, calls=%fused_computation.120 | loop fusion | flops 58368 | bytes 66788 | tf_op jit(solution)/shard_map/jit(_take)/gather | solution.py:27
  136.6 5.1 gather_fusion.1
  141.6 2.2 copy.75
  143.9 263.8 %all-reduce.8.cloned.1.call-done = (bf16[256,400]{1,0:T(8,128)(2,1)}, bf16[256,400]{1,0:T(8,128)(2,1)}) async-done(((bf16[256,400]{1,0:T(8,128)(2,1)}, bf16[256,400]{1,0:T(8,128)(2,1)}), (bf16[256,400]{1,0:T(8,128)(2,1)}, bf16[256,400]{1,0:T(8,128)(2,1)})) %all-reduce.8.cloned.1.call-update) | async-done | bytes 409616 | tf_op jit(solution)/shard_map/psum | solution.py:9
  407.6 1.9 pad_maximum_fusion
  409.5 1.4 copy.74
  410.9 15.8 %while.18 = (s32[]{:T(128)}, f32[512,400]{0,1:T(8,128)S(1)}, bf16[2,512,400]{1,2,0:T(8,128)(2,1)}, f32[2,512,400]{1,2,0:T(8,128)}, bf16[2,512,400]{1,2,0:T(8,128...) while((s32[]{:T(128)}, f32[512,400]{0,1:T(8,128)S(1)}, ...), condition=%wide.region_6.7_spmd.clone, body=%wide.region_2.6_spmd.clone.sunk | while | flops 633964544 | bytes 35072312 | solution.py:70
  411.0 1.2 fusion.56
  412.1 1.5 fusion.55
  413.6 0.2 fusion.57
  413.9 0.6 convolution_add_fusion.3
  414.4 0.4 copy-done.1
  414.9 0.3 copy-done.2
  415.1 0.2 copy-done.8
  415.4 0.4 fusion.58
  415.8 1.0 copy-done.4
  416.9 0.8 copy-done.9
  417.7 1.2 copy-done.5
  418.9 1.1 fusion.56
  420.0 1.5 fusion.55
  421.5 0.2 fusion.57
  421.8 0.6 convolution_add_fusion.3
  422.3 0.4 copy-done.1
  422.8 0.3 copy-done.2
  423.0 0.2 copy-done.8
  423.3 0.4 fusion.58
  423.7 1.0 copy-done.4
  424.8 0.8 copy-done.9
  425.6 1.2 copy-done.5
  426.8 2.2 copy.76
  429.0 41.5 %all_to_all.22 = bf16[16,4,16,400]{3,2,1,0:T(8,128)(2,1)S(1)} all-to-all(bf16[16,4,16,400]{3,2,1,0:T(8,128)(2,1)} %bitcast.147), channel_id=1, replica_groups=mesh['src'=16,'dst'=32] {'src'}, dimensions={0} | all-to-all | bytes 1638400 | tf_op jit(solution)/shard_map/all_to_all | solution.py:73
  470.5 0.7 fusion.24
  471.2 0.3 copy-done.7
  471.5 1.1 copy.78
  472.6 17.1 %all-to-all-start.3 = ((bf16[16,4,16,400]{3,2,1,0:T(8,128)(2,1)}), bf16[16,4,16,400]{3,2,1,0:T(8,128)(2,1)}, u32[]{:S(2)}, u32[]{:S(2)}) async-start(bf16[16,4,16,400]{3,2,1,0:T(8,128)(2,1)} %copy.78), calls=%async_computation.3 | async-start | bytes 2097152 | tf_op jit(solution)/shard_map/all_to_all | solution.py:13
  489.7 0.8 convert_element_type.81
  491.8 2.9 copy.86
  494.7 284.3 %all-reduce.6.cloned.1.call-done = bf16[512,400]{0,1:T(8,128)(2,1)} async-done(((bf16[512,400]{0,1:T(8,128)(2,1)}), bf16[512,400]{0,1:T(8,128)(2,1)}) %all-reduce.6.cloned.1.call-update) | async-done | bytes 409616 | tf_op jit(solution)/shard_map/psum | solution.py:93
  779.0 1.1 convert_element_type.82
  780.1 0.2 copy.81
  780.3 7.5 scatter_fusion
  787.8 110.7 %all-reduce.9 = bf16[256,400]{1,0:T(8,128)(2,1)S(1)} all-reduce(f32[256,400]{1,0:T(8,128)S(1)} %scatter_fusion), channel_id=1, replica_groups=mesh['src'=16,'dst'=32] {'src'}, use_global_device_ids=true, to_apply=%region_11.12 | all-reduce | flops 102400 | bytes 614400 | tf_op jit(solution)/shard_map/psum | solution.py:103
  898.6 0.8 copy.84
  899.4 3.3 bitcast_convert_fusion
  902.7 7.3 scatter_custom_fusion
  910.1 137.6 %all-reduce.10 = bf16[256,400]{1,0:T(8,128)(2,1)S(1)} all-reduce(f32[256,400]{1,0:T(8,128)S(1)} %scatter_custom_fusion), channel_id=1, replica_groups=mesh['src'=16,'dst'=32] {'dst'}, use_global_device_ids=true, to_apply=%region_8.9 | all-reduce | flops 102400 | bytes 614400 | tf_op jit(solution)/shard_map/psum | solution.py:91
  1047.6 0.8 copy.83
  (51 shorter events, 0.6 us)
Async XLA Ops:
  7.2 71.1 %copy-start = (bf16[4,400,400]{2,1,0:T(8,128)(2,1)S(1)}, bf16[4,400,400]{2,1,0:T(8,128)(2,1)}, u32[]{:S(2)}) copy-start(bf16[4,400,400]{2,1,0:T(8,128)(2,1)} %param.11) | copy-start | bytes 3840004
  78.3 1.0 copy-start.6
  79.3 10.7 %copy-start.13 = (s32[1,2]{1,0:T(1,128)S(1)}, s32[1,2]{1,0:T(1,128)}, u32[]{:S(2)}) copy-start(s32[1,2]{1,0:T(1,128)} %param.17) | copy-start | bytes 28
  79.3 12.5 %copy-start.10 = (bf16[256,400]{0,1:T(8,128)(2,1)S(1)}, bf16[256,400]{0,1:T(8,128)(2,1)}, u32[]{:S(2)}) copy-start(bf16[256,400]{0,1:T(8,128)(2,1)} %param.13) | copy-start | bytes 614404
  80.4 12.5 %copy-start.3 = (s32[1,1,64]{2,1,0:T(1,128)S(1)}, s32[1,1,64]{2,1,0:T(1,128)}, u32[]{:S(2)}) copy-start(s32[1,1,64]{2,1,0:T(1,128)} %param.16) | copy-start | bytes 772
  80.4 15.4 %copy-start.12 = (s32[8,128]{1,0:T(8,128)S(1)}, s32[8,128]{1,0:T(8,128)}, u32[]{:S(2)}) copy-start(s32[8,128]{1,0:T(8,128)} %constant.161.clone.1) | copy-start | bytes 12292
  80.4 329.1 %all-to-all-start.1 = ((bf16[16,4,16,400]{3,2,1,0:T(8,128)(2,1)}), bf16[16,4,16,400]{3,2,1,0:T(8,128)(2,1)}, u32[]{:S(2)}, u32[]{:S(2)}) async-start(bf16[16,4,16,400]{3,2,1,0:T(8,128)(2,1)} %copy.70), calls=%async_computation.1 | async-start | bytes 2097152 | tf_op jit(solution)/shard_map/all_to_all | solution.py:35
  89.9 46.6 %copy-start.11 = (s32[1,1,1024]{2,1,0:T(1,128)S(1)}, s32[1,1,1024]{2,1,0:T(1,128)}, u32[]{:S(2)}) copy-start(s32[1,1,1024]{2,1,0:T(1,128)} %param.15) | copy-start | bytes 12292
  89.9 317.7 %all-reduce.8.cloned.1.call-start = ((), (), s32[]{:S(2)}) async-start(), calls=%async_computation.5 | async-start | bytes 1048576 | tf_op jit(solution)/shard_map/psum | solution.py:9
  413.8 1.0 copy-start.1
  413.8 1.3 copy-start.2
  413.8 1.5 copy-start.8
  415.4 1.4 copy-start.4
  416.8 0.9 copy-start.9
  417.7 1.2 copy-start.5
  421.7 1.0 copy-start.1
  421.7 1.3 copy-start.2
  421.7 1.5 copy-start.8
  423.3 1.4 copy-start.4
  424.7 0.9 copy-start.9
  425.6 1.2 copy-start.5
  470.5 1.0 copy-start.7
  472.6 430.1 %all-to-all-start.3 = ((bf16[16,4,16,400]{3,2,1,0:T(8,128)(2,1)}), bf16[16,4,16,400]{3,2,1,0:T(8,128)(2,1)}, u32[]{:S(2)}, u32[]{:S(2)}) async-start(bf16[16,4,16,400]{3,2,1,0:T(8,128)(2,1)} %copy.78), calls=%async_computation.3 | async-start | bytes 2097152 | tf_op jit(solution)/shard_map/all_to_all | solution.py:13
  489.7 289.3 %all-reduce.6.cloned.1.call-start = ((), (), s32[]{:S(2)}) async-start(), calls=%async_computation.4 | async-start | bytes 819200 | tf_op jit(solution)/shard_map/psum | solution.py:93
Sparse Core Ops, SparseCore 0:
  93.7 313.8 all-reduce.7
  493.4 285.5 all-reduce.5
where the time goes:
time: 1060 us
  waiting for transfers between devices  548 us (52%)
  blocking collectives  354 us (33%)
  other arithmetic  64 us (6%)
  local copies, waits for them, and re-layouts  35.9 us (3%)
  starting transfers between devices  26.7 us (3%)
  between operations  16.7 us (2%)
    psum x1, waiting for transfers between devices, body(): lax.psum(span_grad.astype(jnp.bfloat16), 'dst').astype(jnp.float32)  284 us
    psum x1, waiting for transfers between devices, from_root(): return lax.psum(block, axis)  264 us
    psum x1, blocking collectives, body(): grad_src = lax.psum(src_local, 'dst').astype(jnp.bfloat16)  138 us
    psum x1, blocking collectives, body(): grad_dst = lax.psum(dst_local, 'src').astype(jnp.bfloat16)  111 us
    all_to_all x1, blocking collectives, body(): lax.all_to_all(inputs, 'src', split_axis=0, concat_axis=0, tiled=True)  64.1 us
    all_to_all x1, blocking collectives, body(): lax.all_to_all(grads_out, 'src', split_axis=0, concat_axis=0, tiled=True)  41.5 us
    gather x3, other arithmetic, body(): jnp.repeat(counts, slot_cap, total_repeat_length=slot_total)  40.7 us
  transfers between devices with their start and end apart: 4, of which 2 were waited for; matrix products, arithmetic and copies ran while one was open for 7% of the time, Pallas kernels for 0%

commit v1 on v0

--- a/solution.py
+++ b/solution.py
@@ -100,7 +100,7 @@
     )
     for index in range(span_total):
         dst_local = dst_local + jnp.where(span_ids[index] == own_index, span_sums[index], 0.0)
-    grad_dst = lax.psum(dst_local, "src").astype(jnp.bfloat16)
+    grad_dst = jnp.sum(lax.all_gather(dst_local, "src"), axis=0).astype(jnp.bfloat16)
     return (grad_rel, grad_src, grad_dst)
 
 

time: 1060 us -> 1090 us (1.028)
  the two profiles are of different devices: /device:TPU:384 before, /device:TPU:6 now
where the time goes in v1:
time: 1090 us
  waiting for transfers between devices  559 us (51%)
  blocking collectives  358 us (33%)
  other arithmetic  66 us (6%)
  starting transfers between devices  43.3 us (4%)
  local copies, waits for them, and re-layouts  31.6 us (3%)
  between operations  16.4 us (2%)
    psum x1, waiting for transfers between devices, body(): lax.psum(span_grad.astype(jnp.bfloat16), 'dst').astype(jnp.float32)  275 us
    psum x1, waiting for transfers between devices, from_root(): return lax.psum(block, axis)  263 us
    psum x1, blocking collectives, body(): grad_src = lax.psum(src_local, 'dst').astype(jnp.bfloat16)  223 us
    all_to_all x1, blocking collectives, body(): lax.all_to_all(inputs, 'src', split_axis=0, concat_axis=0, tiled=True)  72 us
    all_to_all x1, blocking collectives, body(): lax.all_to_all(grads_out, 'src', split_axis=0, concat_axis=0, tiled=True)  63.3 us
    gather x3, other arithmetic, body(): jnp.repeat(counts, slot_cap, total_repeat_length=slot_total)  40.7 us
    all_to_all x1, starting transfers between devices, send_back(): lax.all_to_all(rows_out, 'src', split_axis=0, concat_axis=0, tiled=True)  36.3 us
  transfers between devices with their start and end apart: 5, of which 3 were waited for; matrix products, arithmetic and copies ran while one was open for 7% of the time, Pallas kernels for 0%

profile of v1, /device:TPU:6, one launch (start us, length us, event | category | flops | bytes accessed | tf_op | source)
XLA Modules:
  0.0 1085.1 jit_solution(3360541493140118327)
XLA Ops:
  7.2 1.2 copy.66
  8.4 0.7 compare_select_fusion.2
  9.1 4.0 gather_fusion
  13.0 72.0 %all_to_all.21 = bf16[16,4,16,400]{3,2,1,0:T(8,128)(2,1)S(1)} all-to-all(bf16[16,4,16,400]{3,2,1,0:T(8,128)(2,1)S(1)} %bitcast.148), channel_id=1, replica_groups=mesh['src'=16,'dst'=32] {'src'}, dimensions={0} | all-to-all | bytes 1638400 | tf_op jit(solution)/shard_map/all_to_all | solution.py:74
  85.0 0.7 fusion.27
  85.7 0.3 copy-done.7
  86.1 1.1 copy.68
  87.2 6.9 all-to-all-start.1
  94.1 0.1 copy.69
  94.3 0.6 fusion.40
  96.1 0.8 broadcast_select_fusion.1
  97.1 5.1 gather_fusion.1
  102.1 2.2 copy.73
  104.3 0.7 fusion.39
  105.0 0.7 fusion.36
  105.7 0.7 fusion.38
  106.5 0.7 fusion.37
  107.3 4.4 compare_select_fusion.3
  111.7 0.7 compare_reduce_fusion.56
  112.4 35.6 %select_select_fusion = s32[1024]{0:T(1024)S(1)} fusion(pred[1024]{0:T(1024)(128)(4,1)S(1)} %get-tuple-element.256, pred[1024]{0:T(1024)(128)(4,1)S(1)} %get-tuple-element.255, pred[1024]{0:T(1024)(128)(4,1)S(1)} %get-tuple-element.254, pred[1024]{0:T(1024)(128)(4,1)S(1)} %get-tuple-element.253, pred[1024]{0:T(1024)(128)(4,1)S(1)} %get-tuple-element.252, ...), kind=kLoop, calls=%fused_computation.120 | loop fusion | flops 58368 | bytes 66788 | tf_op jit(solution)/shard_map/jit(_take)/gather | solution.py:27
  148.0 262.9 %all-reduce.7.cloned.1.call-done = (bf16[256,400]{1,0:T(8,128)(2,1)}, bf16[256,400]{1,0:T(8,128)(2,1)}) async-done(((bf16[256,400]{1,0:T(8,128)(2,1)}, bf16[256,400]{1,0:T(8,128)(2,1)}), (bf16[256,400]{1,0:T(8,128)(2,1)}, bf16[256,400]{1,0:T(8,128)(2,1)})) %all-reduce.7.cloned.1.call-update) | async-done | bytes 409616 | tf_op jit(solution)/shard_map/psum | solution.py:9
  410.9 1.9 pad_maximum_fusion
  412.8 1.4 copy.72
  414.2 10.8 while.18
  414.3 1.6 fusion.55
  415.8 0.1 fusion.56
  416.0 0.2 fusion.57
  416.2 0.6 convolution_add_fusion.3
  416.8 0.4 copy-done.2
  417.2 0.3 copy-done.9
  417.5 0.4 fusion.58
  418.0 0.4 copy-done.5
  418.5 0.4 copy-done.10
  418.9 0.8 copy-done.6
  419.6 1.6 fusion.55
  421.2 0.1 fusion.56
  421.4 0.2 fusion.57
  421.6 0.6 convolution_add_fusion.3
  422.2 0.4 copy-done.2
  422.6 0.3 copy-done.9
  422.9 0.4 fusion.58
  423.3 0.4 copy-done.5
  423.8 0.4 copy-done.10
  424.2 0.7 copy-done.6
  425.0 0.8 convert_element_type.81
  427.1 2.9 copy.84
  429.9 275.1 %all-reduce.5.cloned.1.call-done = bf16[512,400]{0,1:T(8,128)(2,1)} async-done(((bf16[512,400]{0,1:T(8,128)(2,1)}), bf16[512,400]{0,1:T(8,128)(2,1)}) %all-reduce.5.cloned.1.call-update) | async-done | bytes 409616 | tf_op jit(solution)/shard_map/psum | solution.py:93
  705.0 1.1 convert_element_type.82
  706.2 0.2 copy.79
  706.4 7.5 scatter_fusion
  713.9 0.8 copy-done.1
  714.7 1.4 copy.74
  716.1 63.3 %all_to_all.22 = bf16[16,4,16,400]{3,2,1,0:T(8,128)(2,1)S(1)} all-to-all(bf16[16,4,16,400]{3,2,1,0:T(8,128)(2,1)S(1)} %bitcast.149), channel_id=1, replica_groups=mesh['src'=16,'dst'=32] {'src'}, dimensions={0} | all-to-all | bytes 1638400 | tf_op jit(solution)/shard_map/all_to_all | solution.py:73
  779.4 0.7 fusion.24
  780.2 0.3 copy-done.8
  780.4 1.1 copy.76
  781.5 36.3 %all-to-all-start.3 = ((bf16[16,4,16,400]{3,2,1,0:T(8,128)(2,1)}), bf16[16,4,16,400]{3,2,1,0:T(8,128)(2,1)S(1)}, u32[]{:S(2)}, u32[]{:S(2)}) async-start(bf16[16,4,16,400]{3,2,1,0:T(8,128)(2,1)} %copy.76), calls=%async_computation.3 | async-start | bytes 2097152 | tf_op jit(solution)/shard_map/all_to_all | solution.py:13
  817.8 3.3 bitcast_convert_fusion
  821.2 21.5 %all-to-all-done.3 = bf16[16,4,16,400]{3,2,1,0:T(8,128)(2,1)S(1)} async-done(((bf16[16,4,16,400]{3,2,1,0:T(8,128)(2,1)}), bf16[16,4,16,400]{3,2,1,0:T(8,128)(2,1)S(1)}, u32[]{:S(2)}, u32[]{:S(2)}) %all-to-all-start.3) | async-done | bytes 819232 | tf_op jit(solution)/shard_map/all_to_all | solution.py:13
  842.6 7.0 scatter_custom_fusion
  849.6 222.9 %all-reduce.8 = bf16[256,400]{1,0:T(8,128)(2,1)S(1)} all-reduce(f32[256,400]{1,0:T(8,128)S(1)} %scatter_custom_fusion), channel_id=1, replica_groups=mesh['src'=16,'dst'=32] {'dst'}, use_global_device_ids=true, to_apply=%region_8.9 | all-reduce | flops 102400 | bytes 614400 | tf_op jit(solution)/shard_map/psum | solution.py:91
  1072.5 0.8 copy.81
  1073.3 4.4 reduce_sum.33
  1077.8 0.8 copy.82
  (56 shorter events, 0.7 us)
Async XLA Ops:
  7.2 77.8 %copy-start = (bf16[4,400,400]{2,1,0:T(8,128)(2,1)S(1)}, bf16[4,400,400]{2,1,0:T(8,128)(2,1)}, u32[]{:S(2)}) copy-start(bf16[4,400,400]{2,1,0:T(8,128)(2,1)} %param.11) | copy-start | bytes 3840004
  85.0 1.1 copy-start.7
  86.1 8.0 copy-start.11
  87.2 7.1 copy-start.14
  87.2 9.8 copy-start.12
  87.2 325.6 %all-to-all-start.1 = ((bf16[16,4,16,400]{3,2,1,0:T(8,128)(2,1)}), bf16[16,4,16,400]{3,2,1,0:T(8,128)(2,1)}, u32[]{:S(2)}, u32[]{:S(2)}) async-start(bf16[16,4,16,400]{3,2,1,0:T(8,128)(2,1)} %copy.68), calls=%async_computation.1 | async-start | bytes 2097152 | tf_op jit(solution)/shard_map/all_to_all | solution.py:35
  94.1 316.8 %all-reduce.7.cloned.1.call-start = ((), (), s32[]{:S(2)}) async-start(), calls=%async_computation.6 | async-start | bytes 1048576 | tf_op jit(solution)/shard_map/psum | solution.py:9
  96.9 608.1 %all-reduce.5.cloned.1.call-start = ((), (), s32[]{:S(2)}) async-start(), calls=%async_computation.4 | async-start | bytes 819200 | tf_op jit(solution)/shard_map/psum | solution.py:93
  102.1 2.2 copy-start.4
  102.1 5.0 copy-start.13
  414.2 1.6 copy-start.3
  416.2 1.0 copy-start.2
  416.2 1.3 copy-start.9
  416.8 1.5 copy-start.5
  418.0 0.9 copy-start.10
  418.4 1.2 copy-start.6
  419.6 1.6 copy-start.3
  421.6 1.0 copy-start.2
  421.6 1.3 copy-start.9
  422.2 1.5 copy-start.5
  423.3 0.9 copy-start.10
  423.8 1.2 copy-start.6
  425.8 647.5 %all-gather.3.cloned.1.call-start = ((), (), s32[]{:S(2)}) async-start(), calls=%async_computation.5 | async-start | bytes 8912896 | tf_op jit(solution)/shard_map/all_gather | solution.py:103
  713.9 0.8 copy-start.1
  779.4 1.0 copy-start.8
  781.5 61.2 %all-to-all-start.3 = ((bf16[16,4,16,400]{3,2,1,0:T(8,128)(2,1)}), bf16[16,4,16,400]{3,2,1,0:T(8,128)(2,1)S(1)}, u32[]{:S(2)}, u32[]{:S(2)}) async-start(bf16[16,4,16,400]{3,2,1,0:T(8,128)(2,1)} %copy.76), calls=%async_computation.3 | async-start | bytes 2097152 | tf_op jit(solution)/shard_map/all_to_all | solution.py:13
Sparse Core Ops, SparseCore 0:
  97.8 313.0 all-reduce.6
  425.9 279.0 all-reduce.4
  714.8 271.3 all-gather.2
